TPU v7x, 32 devices: a whole 2x2x4 slice. The times are simulated.
32 devices in a mesh: slab: 8 (over y, x, core), pencil: 4 (over z).
Axes of the slice: x: 2, y: 2, z: 4, core: 2. Of those that a mesh axis runs over, the one named last changes fastest.
Arguments:
- descriptors: bfloat16 [49152, 1600], P(('slab', 'pencil')), may hold values from -6 to 6
- species: int32 [49152], P(('slab', 'pencil')), may hold values from 0 to 3
- bucket_count: int32 [128], P(('slab', 'pencil')), may hold values from 288 to 384, as said below
- base_index: int32 [3, 49152], P(None, ('slab', 'pencil')), may hold values from 0 to 383, as said below
- fraction: float32 [3, 49152], P(None, ('slab', 'pencil')), may hold values from 0 to 0.999
- weight_in: bfloat16 [1600, 256], replicated, may hold values from -0.15625 to 0.15625
- bias_in: float32 [256], replicated, may hold values from -4 to 4
- weight_mid: bfloat16 [2, 256, 256], replicated, may hold values from -0.375 to 0.375
- bias_mid: float32 [2, 256], replicated, may hold values from -4 to 4
- weight_out: bfloat16 [3, 256], replicated, may hold values from -0.0390625 to 0.0390625
- bias_out: float32 [3], replicated, may hold values from -0.2 to 0.2
Outputs:
- energy: float32 [], replicated
- site_forces: float32 [2, 3, 49152], P(None, None, ('slab', 'pencil'))
- descriptor_grad: bfloat16 [49152, 1600], P(('slab', 'pencil'))
Inputs may be any that keep to these rules, and one draw needn't show every extreme that they name: Slot i is in use when i % 384 < bucket_count[i // 384]. Among the buckets of every device at least one is full. Slots come in blocks of 1536; block d belongs to slab index d // 4 and pencil index d % 4. base_index[0, i] lies in that slab's planes, within the 4 planes of the slot's bucket (bucket b covers that slab's planes (b % 4) * 4 onwards); base_index[1, i] lies in that pencil's 48 rows; base_index[2, i] is any column.
All inputs are finite; a program needn't handle non-finite values.
Results may differ from a plain program's by a relative error of at most 0.018.
Values sent between devices are 32-bit elements; how exact they have to be, the bound alone decides.
No kernel may reach another device: no remote copies, remote signals or barrier semaphores. Data moves between devices by JAX's collectives and lax.ppermute only.
A program may use at most 192 MiB of HBM per device.

v0:
```python
import math
import jax
import jax.numpy as jnp
from jax import lax
from jax.sharding import PartitionSpec as P

NX = 384
CZ = 16
CY = 48
BZ = 4
ion_table = (6.0, 1.0, 9.0, 7.0)
wannier_table = (-8.0, 0.0, -8.0, -8.0)
spline_coeffs = (1.0 / 120.0, 26.0 / 120.0, 66.0 / 120.0, 26.0 / 120.0, 1.0 / 120.0)
ewald_beta = 1.4
shift_scale = 0.9
highest = lax.Precision.HIGHEST


def extended(cells, sides, width):
    for axis, dim in sides:
        count = lax.axis_size(axis)
        head = lax.slice_in_dim(cells, 0, width, axis=dim)
        tail = lax.slice_in_dim(cells, cells.shape[dim] - width, cells.shape[dim], axis=dim)
        cells = jnp.concatenate(
            [
                lax.ppermute(tail, axis, [(i, (i + 1) % count) for i in range(count)]),
                cells,
                lax.ppermute(head, axis, [((i + 1) % count, i) for i in range(count)]),
            ],
            axis=dim,
        )
    return cells


def bspline(offset):
    folded = jnp.minimum(offset, 6.0 - offset)
    part_one = jnp.maximum(folded, 0.0)
    part_two = jnp.maximum(folded - 1.0, 0.0)
    part_three = jnp.maximum(folded - 2.0, 0.0)
    spline_val = (part_one**5 - 6.0 * part_two**5 + 15.0 * part_three**5) / 120.0
    spline_slope = (part_one**4 - 6.0 * part_two**4 + 15.0 * part_three**4) / 24.0
    return (spline_val, jnp.where(offset <= 3.0, spline_slope, -spline_slope))


def species_charge(species, charge_list):
    kind_ids = jnp.arange(len(charge_list), dtype=jnp.int32)
    levels = jnp.asarray(charge_list, jnp.float32)
    picked = jnp.where(species[None, :] == kind_ids[:, None], levels[:, None], 0.0)
    return jnp.sum(picked, axis=0)


def fitting(descriptors, weight_in, bias_in, weight_mid, bias_mid, weight_out, bias_out):
    hidden = jnp.tanh(
        jnp.dot(descriptors, weight_in, preferred_element_type=jnp.float32) + bias_in
    ).astype(jnp.bfloat16)
    for layer_idx in range(weight_mid.shape[0]):
        pre_act = (
            jnp.dot(hidden, weight_mid[layer_idx], preferred_element_type=jnp.float32)
            + bias_mid[layer_idx]
        )
        hidden = (hidden.astype(jnp.float32) + jnp.tanh(pre_act)).astype(jnp.bfloat16)
    output_raw = lax.dot_general(
        weight_out, hidden, (((1,), (1,)), ((), ())), preferred_element_type=jnp.float32
    )
    return shift_scale * jnp.tanh(output_raw + bias_out[:, None])


def axis_terms(index, length):
    signed = jnp.where(2 * index >= length, index - length, index).astype(jnp.float32) / length
    orders = jnp.arange(1, 6, dtype=jnp.int32)
    phases = (index[:, None] * orders[None, :] % length).astype(jnp.float32) * (
        2.0 * math.pi / length
    )
    coeffs = jnp.asarray(spline_coeffs, jnp.float32)
    real_sum = jnp.sum(coeffs[None, :] * jnp.cos(phases), axis=1)
    imag_sum = jnp.sum(coeffs[None, :] * jnp.sin(phases), axis=1)
    modulus = 1.0 / (real_sum * real_sum + imag_sum * imag_sum)
    damping = jnp.exp(-((math.pi / ewald_beta) ** 2) * signed * signed)
    return (signed * signed, damping * modulus)


def influence(z_index, z_len, y_index, y_len, x_index, x_len):
    z_sq, z_fac = axis_terms(z_index, z_len)
    y_sq, y_fac = axis_terms(y_index, y_len)
    x_sq, x_fac = axis_terms(x_index, x_len)
    squared = z_sq[:, None, None] + y_sq[None, :, None] + x_sq[None, None, :]
    safe_sq = jnp.where(squared > 0.0, squared, 1.0)
    volume = float(z_len * y_len * x_len)
    scaled = (
        z_fac[:, None, None]
        * y_fac[None, :, None]
        * x_fac[None, None, :]
        / (math.pi * volume * safe_sq)
    )
    return jnp.where(squared > 0.0, scaled, 0.0)


def dft_table(length):
    index = jnp.arange(length, dtype=jnp.int32)
    angles = (index[:, None] * index[None, :] % length).astype(jnp.float32) * (
        2.0 * math.pi / length
    )
    return (jnp.cos(angles), jnp.sin(angles))


def half_table(length, width):
    positions = jnp.arange(length, dtype=jnp.int32)
    wave_ids = jnp.arange(width, dtype=jnp.int32)
    angles = (positions[:, None] * wave_ids[None, :] % length).astype(jnp.float32) * (
        2.0 * math.pi / length
    )
    kept_mask = (2 * wave_ids <= length).astype(jnp.float32)
    doubled = (
        jnp.where((wave_ids == 0) | (2 * wave_ids == length), 1.0, 2.0).astype(jnp.float32)
        * kept_mask
    )
    return (jnp.cos(angles) * kept_mask[None, :], jnp.sin(angles) * kept_mask[None, :], doubled)


def dense_window(relative, start, length):
    steps_idx = jnp.arange(8, dtype=jnp.int32)
    spline_val, spline_slope = bspline(
        relative[:, None] - steps_idx.astype(jnp.float32)[None, :] + 6.0
    )
    cell_ids = jnp.arange(length, dtype=jnp.int32)
    target = (start[:, None] + steps_idx[None, :]) % length
    matches = target[:, :, None] == cell_ids[None, None, :]
    dense_val = jnp.sum(jnp.where(matches, spline_val[:, :, None], 0.0), axis=1)
    dense_slope = jnp.sum(jnp.where(matches, spline_slope[:, :, None], 0.0), axis=1)
    return (dense_val, dense_slope)


def lead_product(table, data, dim):
    return lax.dot_general(table, data, (((1,), (dim,)), ((), ())), precision=highest)


def forward_pair(cosine, sine, real_part, imag_part, dim):
    real_cos = lead_product(cosine, real_part, dim)
    imag_sin = lead_product(sine, imag_part, dim)
    imag_cos = lead_product(cosine, imag_part, dim)
    real_sin = lead_product(sine, real_part, dim)
    return (real_cos + imag_sin, imag_cos - real_sin)


def inverse_pair(cosine, sine, real_part, imag_part, dim):
    real_cos = lead_product(cosine, real_part, dim)
    imag_sin = lead_product(sine, imag_part, dim)
    imag_cos = lead_product(cosine, imag_part, dim)
    real_sin = lead_product(sine, real_part, dim)
    return (real_cos - imag_sin, real_sin + imag_cos)


def body(
    descriptors,
    species,
    bucket_count,
    base_index,
    fraction,
    weight_in,
    bias_in,
    weight_mid,
    bias_mid,
    weight_out,
    bias_out,
):
    n_slab = lax.axis_size("slab")
    n_pencil = lax.axis_size("pencil")
    slab_idx = lax.axis_index("slab")
    pencil_idx = lax.axis_index("pencil")
    rows_all = CY * n_pencil
    planes_all = CZ * n_slab
    row_part = rows_all // n_slab
    half_cols = NX // 2 + 1
    wave_cols = -(-half_cols // n_pencil) * n_pencil
    column_part = wave_cols // n_pencil
    n_buckets = bucket_count.shape[0]
    capacity = species.shape[0] // n_buckets
    site_count = 2 * capacity
    slot_ids = jnp.arange(capacity, dtype=jnp.int32)
    in_use = (slot_ids[None, :] < bucket_count[:, None]).reshape(-1).astype(jnp.float32)
    charges = (
        jnp.stack([species_charge(species, ion_table), species_charge(species, wannier_table)])
        * in_use[None, :]
    )

    def network(features):
        return fitting(features, weight_in, bias_in, weight_mid, bias_mid, weight_out, bias_out)

    centroid_shift, pullback = jax.vjp(network, descriptors)
    relative = jnp.stack([fraction, fraction + centroid_shift])
    anchor = jnp.stack([slab_idx * CZ, pencil_idx * CY, jnp.zeros((), jnp.int32)])
    local_base = base_index - anchor[:, None]
    site_charge = (
        charges.reshape(2, n_buckets, capacity).transpose(1, 0, 2).reshape(n_buckets, site_count)
    )
    site_rel = (
        relative.reshape(2, 3, n_buckets, capacity)
        .transpose(2, 1, 0, 3)
        .reshape(n_buckets, 3, site_count)
    )
    site_base = jnp.broadcast_to(
        local_base.reshape(3, n_buckets, 1, capacity), (3, n_buckets, 2, capacity)
    )
    site_base = site_base.transpose(1, 0, 2, 3).reshape(n_buckets, 3, site_count)
    bucket_ids = jnp.arange(n_buckets, dtype=jnp.int32)
    window_shape = (BZ + 8, CY + 8, NX)
    zero_index = jnp.zeros((), jnp.int32)

    def spread_step(grid_now, inputs):
        bucket, charge, rel_pos, base_pos = inputs
        plane_val, plane_slope = dense_window(rel_pos[0], base_pos[0] - bucket * BZ + 1, BZ + 8)
        row_val, row_slope = dense_window(rel_pos[1], base_pos[1] + 1, CY + 8)
        col_val, col_slope = dense_window(rel_pos[2], base_pos[2] - 3, NX)
        outer_prod = ((charge[:, None] * plane_val)[:, :, None] * row_val[:, None, :]).reshape(
            site_count, -1
        )
        block_sum = lax.dot_general(
            outer_prod, col_val, (((0,), (0,)), ((), ())), precision=highest
        )
        corner = (bucket * BZ, zero_index, zero_index)
        current = lax.dynamic_slice(grid_now, corner, window_shape)
        grid_now = lax.dynamic_update_slice(
            grid_now, current + block_sum.reshape(window_shape), corner
        )
        return (grid_now, (plane_val, plane_slope, row_val, row_slope, col_val, col_slope))

    charge_grid, windows = lax.scan(
        spread_step,
        jnp.zeros((CZ + 8, CY + 8, NX), jnp.float32),
        (bucket_ids, site_charge, site_rel, site_base),
    )
    half_cos, half_sin, doubled = half_table(NX, wave_cols)
    forward_rows = jnp.stack([half_cos.T, -half_sin.T], axis=1).reshape(2 * wave_cols, NX)
    inverse_rows = jnp.stack(
        [(half_cos * doubled[None, :]).T, (-half_sin * doubled[None, :]).T], axis=0
    )
    row_cos, row_sin = dft_table(rows_all)
    plane_cos, plane_sin = dft_table(planes_all)
    rim_planes = jnp.concatenate([charge_grid[:4], charge_grid[CZ + 4 :]], axis=0)
    arrived = extended(rim_planes, (("slab", 0),), 4)
    inner_grid = charge_grid[4 : CZ + 4].at[:4].add(arrived[:4]).at[CZ - 4 :].add(arrived[12:])
    rim_rows = jnp.concatenate([inner_grid[:, :4], inner_grid[:, CY + 4 :]], axis=1)
    arrived = extended(rim_rows, (("pencil", 1),), 4)
    source_grid = (
        inner_grid[:, 4 : CY + 4].at[:, :4].add(arrived[:, :4]).at[:, CY - 4 :].add(arrived[:, 12:])
    )
    plane_here = source_grid.shape[0]
    row_here = source_grid.shape[1]
    spectrum = lead_product(forward_rows, source_grid, 2).reshape(
        wave_cols, 2, plane_here, row_here
    )
    spectrum = lax.all_to_all(spectrum, "pencil", split_axis=0, concat_axis=3, tiled=True)
    real_y, imag_y = forward_pair(row_cos, row_sin, spectrum[:, 0], spectrum[:, 1], 2)
    spectrum = jnp.stack([real_y, imag_y], axis=1)
    spectrum = lax.all_to_all(spectrum, "slab", split_axis=0, concat_axis=3, tiled=True)
    real_z, imag_z = forward_pair(plane_cos, plane_sin, spectrum[:, 0], spectrum[:, 1], 2)
    x_ids = pencil_idx * column_part + jnp.arange(column_part, dtype=jnp.int32)
    factor = influence(
        jnp.arange(planes_all, dtype=jnp.int32),
        planes_all,
        slab_idx * row_part + jnp.arange(row_part, dtype=jnp.int32),
        rows_all,
        x_ids,
        NX,
    )
    weighted_real = real_z * factor
    weighted_imag = imag_z * factor
    power = weighted_real * real_z + weighted_imag * imag_z
    x_weight = jnp.where((x_ids == 0) | (2 * x_ids == NX), 1.0, 2.0).astype(jnp.float32)
    x_weight = x_weight * (2 * x_ids <= NX).astype(jnp.float32)
    energy_terms = 0.5 * jnp.sum(power * x_weight)
    energy_sum = lax.psum(energy_terms, ("slab", "pencil"))
    back_real, back_imag = inverse_pair(plane_cos, plane_sin, weighted_real, weighted_imag, 0)
    returned = jnp.stack([back_real, back_imag], axis=1)
    returned = lax.all_to_all(returned, "slab", split_axis=0, concat_axis=2, tiled=True)
    back_real, back_imag = inverse_pair(row_cos, row_sin, returned[:, 0], returned[:, 1], 1)
    returned = jnp.stack([back_real, back_imag], axis=1)
    returned = lax.all_to_all(returned, "pencil", split_axis=0, concat_axis=3, tiled=True)
    potential = lax.dot_general(
        returned, inverse_rows, (((1, 3), (0, 1)), ((), ())), precision=highest
    )
    potential = extended(potential, (("slab", 1), ("pencil", 0)), 4)

    def sample_step(inputs):
        bucket, plane_val, plane_slope, row_val, row_slope, col_val, col_slope = inputs
        corner = (zero_index, bucket * BZ, zero_index)
        patch = lax.dynamic_slice(potential, corner, (CY + 8, BZ + 8, NX)).reshape(-1, NX)
        stacked = jnp.concatenate([col_val, col_slope], axis=0)
        both = lax.dot_general(stacked, patch, (((1,), (1,)), ((), ())), precision=highest)
        along = both[:site_count].reshape(site_count, CY + 8, BZ + 8)
        across = both[site_count:].reshape(site_count, CY + 8, BZ + 8)
        site_level = jnp.einsum("sz,sy,syz->s", plane_val, row_val, along, precision=highest)
        grad_z = jnp.einsum("sz,sy,syz->s", plane_slope, row_val, along, precision=highest)
        grad_y = jnp.einsum("sz,sy,syz->s", plane_val, row_slope, along, precision=highest)
        grad_x = jnp.einsum("sz,sy,syz->s", plane_val, row_val, across, precision=highest)
        return (site_level, jnp.stack([grad_z, grad_y, grad_x]))

    levels, slopes = lax.map(sample_step, (bucket_ids,) + tuple(windows))
    forces = -site_charge[:, None, :] * slopes
    site_forces = forces.reshape(n_buckets, 3, 2, capacity).transpose(2, 1, 0, 3).reshape(2, 3, -1)
    (descriptor_grad,) = pullback(-site_forces[1])
    total_slots = species.shape[0] * n_slab * n_pencil
    energy = energy_sum / float(total_slots)
    return (energy, site_forces, descriptor_grad)


def solution(mesh):
    in_specs = (
        P(("slab", "pencil"), None),
        P(("slab", "pencil")),
        P(("slab", "pencil")),
        P(None, ("slab", "pencil")),
        P(None, ("slab", "pencil")),
        P(),
        P(),
        P(),
        P(),
        P(),
        P(),
    )
    out_specs = (P(), P(None, None, ("slab", "pencil")), P(("slab", "pencil"), None))
    return jax.shard_map(body, mesh=mesh, in_specs=in_specs, out_specs=out_specs, check_vma=False)
```

profile of v0, /device:TPU:12, one launch (start us, length us, event | category | flops | bytes accessed | tf_op | source)
XLA Modules:
  0.0 749.2 jit_solution(451744507878971859)
XLA Ops:
  2.3 4.1 fusion.52
  13.4 99.9 %while.39 = (s32[]{:T(128)}, f32[24,56,384]{2,1,0:T(8,128)}, f32[4,768,12]{1,2,0:T(8,128)S(1)}, f32[4,768,12]{1,2,0:T(8,128)}, f32[4,768,56]{1,2,0:T(8,128)}, /*...) while((s32[]{:T(128)}, f32[24,56,384]{2,1,0:T(8,128)}, ...), condition=%wide.region_9.10_spmd, body=%wide.region_2.9_spmd.sunk | while | flops 2392848384 | bytes 12563475 | solution.py:227
  15.5 13.0 %select_reduce_fusion.11 = (f32[768,384]{1,0:T(8,128)S(1)}, f32[768,384]{1,0:T(8,128)S(1)}) fusion(f32[768,8]{1,0:T(8,128)S(1)} %copy.162, s32[768,8]{1,0:T(8,128)S(1)} %copy.163, f32[768,8]{1,0:T(8,128)S(1)} %copy.164), kind=kLoop, calls=%fused_computation.17.clone.1 | loop fusion | flops 11206656 | bytes 2433024 | tf_op jit(solution)/shard_map/while/body/eval_jaxpr/reduce_sum | solution.py:129
  31.3 5.6 fusion.357
  40.4 13.0 %select_reduce_fusion.11 = (f32[768,384]{1,0:T(8,128)S(1)}, f32[768,384]{1,0:T(8,128)S(1)}) fusion(f32[768,8]{1,0:T(8,128)S(1)} %copy.162, s32[768,8]{1,0:T(8,128)S(1)} %copy.163, f32[768,8]{1,0:T(8,128)S(1)} %copy.164), kind=kLoop, calls=%fused_computation.17.clone.1 | loop fusion | flops 11206656 | bytes 2433024 | tf_op jit(solution)/shard_map/while/body/eval_jaxpr/reduce_sum | solution.py:129
  56.3 5.6 fusion.357
  65.4 13.0 %select_reduce_fusion.11 = (f32[768,384]{1,0:T(8,128)S(1)}, f32[768,384]{1,0:T(8,128)S(1)}) fusion(f32[768,8]{1,0:T(8,128)S(1)} %copy.162, s32[768,8]{1,0:T(8,128)S(1)} %copy.163, f32[768,8]{1,0:T(8,128)S(1)} %copy.164), kind=kLoop, calls=%fused_computation.17.clone.1 | loop fusion | flops 11206656 | bytes 2433024 | tf_op jit(solution)/shard_map/while/body/eval_jaxpr/reduce_sum | solution.py:129
  81.3 5.6 fusion.357
  90.4 13.0 %select_reduce_fusion.11 = (f32[768,384]{1,0:T(8,128)S(1)}, f32[768,384]{1,0:T(8,128)S(1)}) fusion(f32[768,8]{1,0:T(8,128)S(1)} %copy.162, s32[768,8]{1,0:T(8,128)S(1)} %copy.163, f32[768,8]{1,0:T(8,128)S(1)} %copy.164), kind=kLoop, calls=%fused_computation.17.clone.1 | loop fusion | flops 11206656 | bytes 2433024 | tf_op jit(solution)/shard_map/while/body/eval_jaxpr/reduce_sum | solution.py:129
  106.3 5.6 fusion.357
  118.7 6.4 collective-permute-done
  140.1 5.4 reshape.1131
  145.5 5.9 all-to-all-start
  151.8 23.2 %all-to-all-done = f32[4,1,75264]{2,1,0:T(1,128)S(1)} async-done(((f32[4,1,75264]{2,1,0:T(1,128)}), f32[4,1,75264]{2,1,0:T(1,128)S(1)}, u32[]{:S(2)}, u32[]{:S(2)}) %all-to-all-start) | async-done | bytes 1204256 | tf_op jit(solution)/shard_map/all_to_all | solution.py:252
  175.5 4.1 reduce.30
  182.8 6.6 copy.150
  189.4 11.7 %all_to_all.55 = f32[49,2,16,192]{3,2,1,0:T(8,128)S(1)} reshape(f32[49,2,16,4,48]{4,3,2,1,0:T(4,128)} %bitcast.337) | data formatting | bytes 2408448 | tf_op jit(solution)/shard_map/all_to_all | solution.py:252
  212.2 5.7 reshape.1133
  217.9 6.0 all-to-all-start.1
  224.2 15.1 %all-to-all-done.1 = f32[8,1,37632]{2,1,0:T(1,128)S(1)} async-done(((f32[8,1,37632]{2,1,0:T(1,128)}), f32[8,1,37632]{2,1,0:T(1,128)S(1)}, u32[]{:S(2)}, u32[]{:S(2)}) %all-to-all-start.1) | async-done | bytes 1204256 | tf_op jit(solution)/shard_map/all_to_all | solution.py:255
  239.3 3.6 reduce.31
  242.9 6.0 reshape.1134
  261.7 3.4 multiply_reduce_fusion.3
  269.5 5.0 reshape.1135
  274.5 19.4 %all_to_all.72 = f32[8,1,37632]{2,1,0:T(1,128)S(1)} all-to-all(f32[8,1,37632]{2,1,0:T(1,128)S(1)} %reshape.1135), channel_id=1, replica_groups=mesh['slab'=8,'pencil'=4] {'slab'}, dimensions={0} | all-to-all | bytes 2408448 | tf_op jit(solution)/shard_map/all_to_all | solution.py:275
  294.0 3.5 reduce.32
  297.5 6.0 reshape.1136
  312.2 3.5 fusion.79
  322.0 5.8 reshape.1137
  327.8 6.8 all-to-all-start.3
  336.6 23.8 %all-to-all-done.3 = f32[4,1,75264]{2,1,0:T(1,128)S(1)} async-done(((f32[4,1,75264]{2,1,0:T(1,128)}), f32[4,1,75264]{2,1,0:T(1,128)S(1)}, u32[]{:S(2)}, u32[]{:S(2)}) %all-to-all-start.3) | async-done | bytes 1204256 | tf_op jit(solution)/shard_map/all_to_all | solution.py:278
  360.5 4.1 reduce.33
  364.6 6.1 reshape.1138
  370.7 6.4 copy.151
  377.1 4.5 all_to_all.67
  381.7 4.1 convolution_bitcast_fusion
  388.6 6.5 collective-permute-done.4
  399.1 44.4 %psum.7 = f32[]{:T(128)} all-reduce(f32[]{:T(128)S(6)} %mul_shard_map.3), channel_id=1, replica_groups=mesh['slab'=8,'pencil'=4] {'slab','pencil'}, use_global_device_ids=true, to_apply=%region_17.18 | all-reduce | flops 1 | bytes 8 | tf_op jit(solution)/shard_map/psum | solution.py:272
  445.8 293.6 %while.40 = (s32[]{:T(128)}, f32[4,3,768]{2,1,0:T(4,128)S(1)}, f32[4,768,12]{1,2,0:T(8,128)}, f32[4,768,56]{1,2,0:T(8,128)}, f32[4,768,384]{2,1,0:T(8,128)}, /*i...) while((s32[]{:T(128)}, f32[4,3,768]{2,1,0:T(4,128)S(1)}, ...), condition=%wide.region_19.20_spmd, body=%wide.region_18.19_spmd.sunk | while | flops 4775567872 | bytes 50012400 | solution.py:298
  450.8 6.7 fusion.366
  462.2 7.0 copy.169
  472.0 12.6 %fusion.369 = f32[768,1,12]{2,1,0:T(1,128)} fusion(f32[768,56,1]{1,2,0:T(1,128)S(1)} %bitcast.322, f32[768,56,12]{1,2,0:T(8,128)} %copy.169), kind=kOutput, calls=%fused_computation.446.clone.1 | convolution fusion | flops 6193152 | bytes 2273280 | tf_op jit(solution)/shard_map/while/body/eval_jaxpr/sz,sy,syz->s/dot_general | solution.py:295
  486.4 7.0 copy.167
  493.6 12.0 %fusion.368 = f32[768,1,12]{2,1,0:T(1,128)S(1)} fusion(f32[768,56,1]{1,2,0:T(1,128)S(1)} %bitcast.325, f32[768,56,12]{1,2,0:T(8,128)} %copy.167), kind=kOutput, calls=%fused_computation.445.clone.1 | convolution fusion | flops 6193152 | bytes 2273280 | tf_op jit(solution)/shard_map/while/body/eval_jaxpr/sz,sy,syz->s/dot_general | solution.py:294
  507.0 12.0 %fusion.370 = f32[768,1,12]{2,1,0:T(1,128)S(1)} fusion(f32[768,56,1]{1,2,0:T(1,128)S(1)} %bitcast.323, f32[768,56,12]{1,2,0:T(8,128)} %copy.167), kind=kOutput, calls=%fused_computation.444.clone.1 | convolution fusion | flops 6193152 | bytes 2273280 | tf_op jit(solution)/shard_map/while/body/eval_jaxpr/sz,sy,syz->s/dot_general | solution.py:293
  524.2 6.7 fusion.366
  535.6 7.0 copy.169
  545.4 12.6 %fusion.369 = f32[768,1,12]{2,1,0:T(1,128)} fusion(f32[768,56,1]{1,2,0:T(1,128)S(1)} %bitcast.322, f32[768,56,12]{1,2,0:T(8,128)} %copy.169), kind=kOutput, calls=%fused_computation.446.clone.1 | convolution fusion | flops 6193152 | bytes 2273280 | tf_op jit(solution)/shard_map/while/body/eval_jaxpr/sz,sy,syz->s/dot_general | solution.py:295
  559.8 7.0 copy.167
  567.0 12.0 %fusion.368 = f32[768,1,12]{2,1,0:T(1,128)S(1)} fusion(f32[768,56,1]{1,2,0:T(1,128)S(1)} %bitcast.325, f32[768,56,12]{1,2,0:T(8,128)} %copy.167), kind=kOutput, calls=%fused_computation.445.clone.1 | convolution fusion | flops 6193152 | bytes 2273280 | tf_op jit(solution)/shard_map/while/body/eval_jaxpr/sz,sy,syz->s/dot_general | solution.py:294
  580.4 12.0 %fusion.370 = f32[768,1,12]{2,1,0:T(1,128)S(1)} fusion(f32[768,56,1]{1,2,0:T(1,128)S(1)} %bitcast.323, f32[768,56,12]{1,2,0:T(8,128)} %copy.167), kind=kOutput, calls=%fused_computation.444.clone.1 | convolution fusion | flops 6193152 | bytes 2273280 | tf_op jit(solution)/shard_map/while/body/eval_jaxpr/sz,sy,syz->s/dot_general | solution.py:293
  597.4 6.7 fusion.366
  608.8 7.0 copy.169
  618.6 12.6 %fusion.369 = f32[768,1,12]{2,1,0:T(1,128)} fusion(f32[768,56,1]{1,2,0:T(1,128)S(1)} %bitcast.322, f32[768,56,12]{1,2,0:T(8,128)} %copy.169), kind=kOutput, calls=%fused_computation.446.clone.1 | convolution fusion | flops 6193152 | bytes 2273280 | tf_op jit(solution)/shard_map/while/body/eval_jaxpr/sz,sy,syz->s/dot_general | solution.py:295
  633.0 7.0 copy.167
  640.2 12.0 %fusion.368 = f32[768,1,12]{2,1,0:T(1,128)S(1)} fusion(f32[768,56,1]{1,2,0:T(1,128)S(1)} %bitcast.325, f32[768,56,12]{1,2,0:T(8,128)} %copy.167), kind=kOutput, calls=%fused_computation.445.clone.1 | convolution fusion | flops 6193152 | bytes 2273280 | tf_op jit(solution)/shard_map/while/body/eval_jaxpr/sz,sy,syz->s/dot_general | solution.py:294
  653.6 12.0 %fusion.370 = f32[768,1,12]{2,1,0:T(1,128)S(1)} fusion(f32[768,56,1]{1,2,0:T(1,128)S(1)} %bitcast.323, f32[768,56,12]{1,2,0:T(8,128)} %copy.167), kind=kOutput, calls=%fused_computation.444.clone.1 | convolution fusion | flops 6193152 | bytes 2273280 | tf_op jit(solution)/shard_map/while/body/eval_jaxpr/sz,sy,syz->s/dot_general | solution.py:293
  670.6 6.7 fusion.366
  682.0 7.0 copy.169
  691.8 12.6 %fusion.369 = f32[768,1,12]{2,1,0:T(1,128)} fusion(f32[768,56,1]{1,2,0:T(1,128)S(1)} %bitcast.322, f32[768,56,12]{1,2,0:T(8,128)} %copy.169), kind=kOutput, calls=%fused_computation.446.clone.1 | convolution fusion | flops 6193152 | bytes 2273280 | tf_op jit(solution)/shard_map/while/body/eval_jaxpr/sz,sy,syz->s/dot_general | solution.py:295
  706.2 7.0 copy.167
  713.4 12.0 %fusion.368 = f32[768,1,12]{2,1,0:T(1,128)S(1)} fusion(f32[768,56,1]{1,2,0:T(1,128)S(1)} %bitcast.325, f32[768,56,12]{1,2,0:T(8,128)} %copy.167), kind=kOutput, calls=%fused_computation.445.clone.1 | convolution fusion | flops 6193152 | bytes 2273280 | tf_op jit(solution)/shard_map/while/body/eval_jaxpr/sz,sy,syz->s/dot_general | solution.py:294
  726.8 12.0 %fusion.370 = f32[768,1,12]{2,1,0:T(1,128)S(1)} fusion(f32[768,56,1]{1,2,0:T(1,128)S(1)} %bitcast.323, f32[768,56,12]{1,2,0:T(8,128)} %copy.167), kind=kOutput, calls=%fused_computation.444.clone.1 | convolution fusion | flops 6193152 | bytes 2273280 | tf_op jit(solution)/shard_map/while/body/eval_jaxpr/sz,sy,syz->s/dot_general | solution.py:293
  742.1 5.5 convolution_convert_fusion
  (320 shorter events, 171.7 us)
Async XLA Ops:
  0.6 1.6 copy-start
  2.3 4.2 copy-start.6
  6.4 1.6 copy-start.3
  8.1 1.6 copy-start.11
  8.1 1.6 copy-start.14
  8.1 1.6 copy-start.18
  8.4 1.2 copy-start.2
  9.6 1.2 copy-start.13
  9.6 1.4 copy-start.16
  9.6 1.4 copy-start.19
  9.6 1.4 copy-start.20
  9.7 1.5 copy-start.21
  13.4 1.9 copy-start.22
  31.3 7.0 copy-start.23
  38.3 1.9 copy-start.22
  56.3 7.0 copy-start.23
  63.3 1.9 copy-start.22
  81.3 7.0 copy-start.23
  88.3 1.9 copy-start.22
  106.2 7.1 copy-start.23
  113.3 5.3 copy-start.8
  114.5 10.5 %collective-permute-start = (f32[4,56,384]{2,1,0:T(8,128)S(1)}, f32[4,56,384]{2,1,0:T(8,128)S(1)}, u32[]{:S(2)}, u32[]{:S(2)}) collective-permute-start(f32[4,56,384]{2,1,0:T(8,128)S(1)} %get-tuple-element.502), channel_id=1, source_target_pairs={{0,4},{4,8},{8,12},{12,16},{16,20},{20,24},{24,28},{28,0},{1,5},{5... | collective-permute-start | bytes 1032200 | tf_op jit(solution)/shard_map/ppermute | solution.py:26
  114.6 11.5 %collective-permute-start.1 = (f32[4,56,384]{2,1,0:T(8,128)S(1)}, f32[4,56,384]{2,1,0:T(8,128)S(1)}, u32[]{:S(2)}, u32[]{:S(2)}) collective-permute-start(f32[4,56,384]{2,1,0:T(8,128)S(1)} %get-tuple-element.501), channel_id=1, source_target_pairs={{4,0},{8,4},{12,8},{16,12},{20,16},{24,20},{28,24},{0,28},{5,1},{9... | collective-permute-start | bytes 1032200 | tf_op jit(solution)/shard_map/ppermute | solution.py:28
  126.2 4.7 collective-permute-start.2
  129.2 4.9 collective-permute-start.3
  145.5 5.9 copy-start.17
  145.5 29.4 %all-to-all-start = ((f32[4,1,75264]{2,1,0:T(1,128)}), f32[4,1,75264]{2,1,0:T(1,128)S(1)}, u32[]{:S(2)}, u32[]{:S(2)}) async-start(f32[4,1,75264]{2,1,0:T(1,128)} %reshape.1131), calls=%async_computation | async-start | bytes 2408448 | tf_op jit(solution)/shard_map/all_to_all | solution.py:252
  217.9 21.4 %all-to-all-start.1 = ((f32[8,1,37632]{2,1,0:T(1,128)}), f32[8,1,37632]{2,1,0:T(1,128)S(1)}, u32[]{:S(2)}, u32[]{:S(2)}) async-start(f32[8,1,37632]{2,1,0:T(1,128)} %reshape.1133), calls=%async_computation.1 | async-start | bytes 2408448 | tf_op jit(solution)/shard_map/all_to_all | solution.py:255
  327.8 32.6 %all-to-all-start.3 = ((f32[4,1,75264]{2,1,0:T(1,128)}), f32[4,1,75264]{2,1,0:T(1,128)S(1)}, u32[]{:S(2)}, u32[]{:S(2)}) async-start(f32[4,1,75264]{2,1,0:T(1,128)} %reshape.1137), calls=%async_computation.3 | async-start | bytes 2408448 | tf_op jit(solution)/shard_map/all_to_all | solution.py:278
  377.1 4.6 copy-start.5
  385.7 13.3 %copy-start.9 = (f32[4,768]{1,0:T(4,128)S(1)}, f32[4,768]{1,0:T(4,128)}, u32[]{:S(2)}) copy-start(f32[4,768]{1,0:T(4,128)} %get-tuple-element.842) | copy-start | bytes 36868
  385.9 9.2 %collective-permute-start.4 = (f32[48,4,384]{2,1,0:T(4,128)S(1)}, f32[48,4,384]{2,1,0:T(4,128)S(1)}, u32[]{:S(2)}, u32[]{:S(2)}) collective-permute-start(f32[48,4,384]{2,1,0:T(4,128)S(1)} %get-tuple-element.509), channel_id=1, source_target_pairs={{0,4},{4,8},{8,12},{12,16},{16,20},{20,24},{24,28},{28,0},{1,5},{5... | collective-permute-start | bytes 884744 | tf_op jit(solution)/shard_map/ppermute | solution.py:26
  385.9 9.1 %collective-permute-start.5 = (f32[48,4,384]{2,1,0:T(4,128)S(1)}, f32[48,4,384]{2,1,0:T(4,128)S(1)}, u32[]{:S(2)}, u32[]{:S(2)}) collective-permute-start(f32[48,4,384]{2,1,0:T(4,128)S(1)} %get-tuple-element.510), channel_id=1, source_target_pairs={{4,0},{8,4},{12,8},{16,12},{20,16},{24,20},{28,24},{0,28},{5,1},{9... | collective-permute-start | bytes 884744 | tf_op jit(solution)/shard_map/ppermute | solution.py:28
  395.1 49.1 %collective-permute-start.6 = (f32[4,24,384]{2,1,0:T(8,128)S(1)}, f32[4,24,384]{2,1,0:T(8,128)S(1)}, u32[]{:S(2)}, u32[]{:S(2)}) collective-permute-start(f32[4,24,384]{2,1,0:T(8,128)S(1)} %get-tuple-element.503), channel_id=1, source_target_pairs={{0,1},{1,2},{2,3},{3,0},{4,5},{5,6},{6,7},{7,4},{8,9},{9,10},{10,1... | collective-permute-start | bytes 442376 | tf_op jit(solution)/shard_map/ppermute | solution.py:26
  396.6 47.6 %collective-permute-start.7 = (f32[4,24,384]{2,1,0:T(8,128)S(1)}, f32[4,24,384]{2,1,0:T(8,128)S(1)}, u32[]{:S(2)}, u32[]{:S(2)}) collective-permute-start(f32[4,24,384]{2,1,0:T(8,128)S(1)} %get-tuple-element.504), channel_id=1, source_target_pairs={{1,0},{2,1},{3,2},{0,3},{5,4},{6,5},{7,6},{4,7},{9,8},{10,9},{11,1... | collective-permute-start | bytes 442376 | tf_op jit(solution)/shard_map/ppermute | solution.py:28
  445.8 293.8 %copy-start.10 = (f32[1536,3]{0,1:T(4,128)S(1)}, f32[1536,3]{0,1:T(4,128)}, u32[]{:S(2)}) copy-start(f32[1536,3]{0,1:T(4,128)} %get-tuple-element.522) | copy-start | bytes 55300
  445.8 293.8 %copy-start.15 = (bf16[3,256]{1,0:T(4,128)(2,1)S(1)}, bf16[3,256]{1,0:T(4,128)(2,1)}, u32[]{:S(2)}) copy-start(bf16[3,256]{1,0:T(4,128)(2,1)} %param.37) | copy-start | bytes 4612
  493.6 13.1 %copy-start.1 = (f32[768,1,12]{2,1,0:T(1,128)S(1)}, f32[768,1,12]{2,1,0:T(1,128)}, u32[]{:S(2)}) copy-start(f32[768,1,12]{2,1,0:T(1,128)} %fusion.369) | copy-start | bytes 110596 | tf_op jit(solution)/shard_map/while
  567.0 13.1 %copy-start.1 = (f32[768,1,12]{2,1,0:T(1,128)S(1)}, f32[768,1,12]{2,1,0:T(1,128)}, u32[]{:S(2)}) copy-start(f32[768,1,12]{2,1,0:T(1,128)} %fusion.369) | copy-start | bytes 110596 | tf_op jit(solution)/shard_map/while
  640.2 13.1 %copy-start.1 = (f32[768,1,12]{2,1,0:T(1,128)S(1)}, f32[768,1,12]{2,1,0:T(1,128)}, u32[]{:S(2)}) copy-start(f32[768,1,12]{2,1,0:T(1,128)} %fusion.369) | copy-start | bytes 110596 | tf_op jit(solution)/shard_map/while
  713.4 13.1 %copy-start.1 = (f32[768,1,12]{2,1,0:T(1,128)S(1)}, f32[768,1,12]{2,1,0:T(1,128)}, u32[]{:S(2)}) copy-start(f32[768,1,12]{2,1,0:T(1,128)} %fusion.369) | copy-start | bytes 110596 | tf_op jit(solution)/shard_map/while
  739.5 2.6 copy-start.12
  740.1 2.1 copy-start.4
  740.1 2.1 copy-start.7
where the time goes:
time: 760 us; the launch traced here: 749 us
  matrix products  254 us (33%)
  local copies, waits for them, and re-layouts  231 us (30%)
  other arithmetic  79.9 us (11%)
  waiting for transfers between devices  79 us (10%)
  blocking collectives  63.9 us (8%)
  starting transfers between devices  29.8 us (4%)
    reduce_sum x12, other arithmetic, dense_window(): jnp.sum(jnp.where(matches, spline_slope[:, :, None], 0.0), axis=1)  53.9 us
    dot_general x4, matrix products, sample_step(): jnp.einsum('sz,sy,syz->s', plane_val, row_val, across, precision=highest)  50.6 us
    dot_general x4, matrix products, sample_step(): jnp.einsum('sz,sy,syz->s', plane_val, row_slope, along, precision=highest)  48.1 us
    dot_general x4, matrix products, sample_step(): jnp.einsum('sz,sy,syz->s', plane_slope, row_val, along, precision=highest)  47.9 us
    unnamed x52, local copies, waits for them, and re-layouts  45 us
    psum x1, blocking collectives, body(): energy_sum = lax.psum(energy_terms, ('slab', 'pencil'))  44.4 us
    reshape x8, local copies, waits for them, and re-layouts, sample_step(): across = both[site_count:].reshape(site_count, CY + 8, BZ + 8)  40.4 us
    dot_general x17, matrix products, lead_product(): lax.dot_general(table, data, (((1,), (dim,)), ((), ())), precision=highest)  39.6 us
  transfers between devices with their start and end apart: 11, of which 7 were waited for; matrix products, arithmetic and copies ran while one was open for 1% of the time, Pallas kernels for 0%

commit v1 on v0

--- a/solution.py
+++ b/solution.py
@@ -272,7 +272,10 @@
     energy_sum = lax.psum(energy_terms, ("slab", "pencil"))
     back_real, back_imag = inverse_pair(plane_cos, plane_sin, weighted_real, weighted_imag, 0)
     returned = jnp.stack([back_real, back_imag], axis=1)
-    returned = lax.all_to_all(returned, "slab", split_axis=0, concat_axis=2, tiled=True)
+    returned = jnp.concatenate(
+        lax.all_to_all(jnp.stack(jnp.split(returned, lax.axis_size("slab"), axis=0)), "slab", 0, 0),
+        axis=2,
+    )
     back_real, back_imag = inverse_pair(row_cos, row_sin, returned[:, 0], returned[:, 1], 1)
     returned = jnp.stack([back_real, back_imag], axis=1)
     returned = lax.all_to_all(returned, "pencil", split_axis=0, concat_axis=3, tiled=True)

time: 760 us -> 788 us (1.037)
  local copies, waits for them, and re-layouts: 231 us -> 254 us
    another operation x0 -> x9, local copies, waits for them, and re-layouts: none -> 17.2 us  [body(): jnp.stack(jnp.split(returned, lax.axis_size('slab'), axis=0))]
    unnamed x52 -> x63, local copies, waits for them, and re-layouts: 45 us -> 52.5 us
where the time goes in v1:
time: 788 us; the launch traced here: 777 us
  local copies, waits for them, and re-layouts  254 us (32%)
  matrix products  254 us (32%)
  other arithmetic  85.2 us (11%)
  waiting for transfers between devices  78.8 us (10%)
  blocking collectives  63.9 us (8%)
  starting transfers between devices  30.1 us (4%)
    reduce_sum x12, other arithmetic, dense_window(): jnp.sum(jnp.where(matches, spline_slope[:, :, None], 0.0), axis=1)  53.9 us
    unnamed x63, local copies, waits for them, and re-layouts  52.5 us
    dot_general x4, matrix products, sample_step(): jnp.einsum('sz,sy,syz->s', plane_val, row_val, across, precision=highest)  50.6 us
    dot_general x4, matrix products, sample_step(): jnp.einsum('sz,sy,syz->s', plane_val, row_slope, along, precision=highest)  48.1 us
    dot_general x4, matrix products, sample_step(): jnp.einsum('sz,sy,syz->s', plane_slope, row_val, along, precision=highest)  47.9 us
    psum x1, blocking collectives, body(): energy_sum = lax.psum(energy_terms, ('slab', 'pencil'))  44.4 us
    reshape x8, local copies, waits for them, and re-layouts, sample_step(): across = both[site_count:].reshape(site_count, CY + 8, BZ + 8)  40.4 us
    dot_general x17, matrix products, lead_product(): lax.dot_general(table, data, (((1,), (dim,)), ((), ())), precision=highest)  39.3 us
  transfers between devices with their start and end apart: 11, of which 7 were waited for; matrix products, arithmetic and copies ran while one was open for 1% of the time, Pallas kernels for 0%

profile of v1, /device:TPU:12, one launch (start us, length us, event | category | flops | bytes accessed | tf_op | source)
XLA Modules:
  0.0 776.7 jit_solution(4481336992775405349)
XLA Ops:
  2.3 4.1 fusion.52
  13.4 100.1 %while.39 = (s32[]{:T(128)}, f32[24,56,384]{2,1,0:T(8,128)}, f32[4,768,12]{1,2,0:T(8,128)S(1)}, f32[4,768,12]{1,2,0:T(8,128)}, f32[4,768,56]{1,2,0:T(8,128)}, /*...) while((s32[]{:T(128)}, f32[24,56,384]{2,1,0:T(8,128)}, ...), condition=%wide.region_9.10_spmd, body=%wide.region_2.9_spmd.sunk | while | flops 2392848384 | bytes 12563475 | solution.py:227
  15.5 13.0 %select_reduce_fusion.11 = (f32[768,384]{1,0:T(8,128)S(1)}, f32[768,384]{1,0:T(8,128)S(1)}) fusion(f32[768,8]{1,0:T(8,128)S(1)} %copy.174, s32[768,8]{1,0:T(8,128)S(1)} %copy.175, f32[768,8]{1,0:T(8,128)S(1)} %copy.176), kind=kLoop, calls=%fused_computation.17.clone.1 | loop fusion | flops 11206656 | bytes 2433024 | tf_op jit(solution)/shard_map/while/body/eval_jaxpr/reduce_sum | solution.py:129
  31.4 5.6 fusion.372
  40.5 13.0 %select_reduce_fusion.11 = (f32[768,384]{1,0:T(8,128)S(1)}, f32[768,384]{1,0:T(8,128)S(1)}) fusion(f32[768,8]{1,0:T(8,128)S(1)} %copy.174, s32[768,8]{1,0:T(8,128)S(1)} %copy.175, f32[768,8]{1,0:T(8,128)S(1)} %copy.176), kind=kLoop, calls=%fused_computation.17.clone.1 | loop fusion | flops 11206656 | bytes 2433024 | tf_op jit(solution)/shard_map/while/body/eval_jaxpr/reduce_sum | solution.py:129
  56.4 5.6 fusion.372
  65.5 13.0 %select_reduce_fusion.11 = (f32[768,384]{1,0:T(8,128)S(1)}, f32[768,384]{1,0:T(8,128)S(1)}) fusion(f32[768,8]{1,0:T(8,128)S(1)} %copy.174, s32[768,8]{1,0:T(8,128)S(1)} %copy.175, f32[768,8]{1,0:T(8,128)S(1)} %copy.176), kind=kLoop, calls=%fused_computation.17.clone.1 | loop fusion | flops 11206656 | bytes 2433024 | tf_op jit(solution)/shard_map/while/body/eval_jaxpr/reduce_sum | solution.py:129
  81.4 5.6 fusion.372
  90.5 13.0 %select_reduce_fusion.11 = (f32[768,384]{1,0:T(8,128)S(1)}, f32[768,384]{1,0:T(8,128)S(1)}) fusion(f32[768,8]{1,0:T(8,128)S(1)} %copy.174, s32[768,8]{1,0:T(8,128)S(1)} %copy.175, f32[768,8]{1,0:T(8,128)S(1)} %copy.176), kind=kLoop, calls=%fused_computation.17.clone.1 | loop fusion | flops 11206656 | bytes 2433024 | tf_op jit(solution)/shard_map/while/body/eval_jaxpr/reduce_sum | solution.py:129
  106.4 5.6 fusion.372
  118.8 6.4 collective-permute-done
  140.2 5.4 reshape.1139
  145.6 5.9 all-to-all-start
  151.9 23.2 %all-to-all-done = f32[4,1,75264]{2,1,0:T(1,128)S(1)} async-done(((f32[4,1,75264]{2,1,0:T(1,128)}), f32[4,1,75264]{2,1,0:T(1,128)S(1)}, u32[]{:S(2)}, u32[]{:S(2)}) %all-to-all-start) | async-done | bytes 1204256 | tf_op jit(solution)/shard_map/all_to_all | solution.py:252
  175.6 4.1 reduce.30
  182.9 6.6 copy.162
  189.5 11.7 %all_to_all.45 = f32[49,2,16,192]{3,2,1,0:T(8,128)S(1)} reshape(f32[49,2,16,4,48]{4,3,2,1,0:T(4,128)} %bitcast.351) | data formatting | bytes 2408448 | tf_op jit(solution)/shard_map/all_to_all | solution.py:252
  212.3 5.7 reshape.1141
  218.0 6.2 all-to-all-start.1
  224.5 14.9 %all-to-all-done.1 = f32[8,1,37632]{2,1,0:T(1,128)S(1)} async-done(((f32[8,1,37632]{2,1,0:T(1,128)}), f32[8,1,37632]{2,1,0:T(1,128)S(1)}, u32[]{:S(2)}, u32[]{:S(2)}) %all-to-all-start.1) | async-done | bytes 1204256 | tf_op jit(solution)/shard_map/all_to_all | solution.py:255
  239.4 3.6 reduce.31
  243.0 6.0 reshape.1142
  267.0 5.5 fusion.92
  297.2 5.0 reshape.1143
  302.2 19.4 %all_to_all.59 = f32[8,1,37632]{2,1,0:T(1,128)S(1)} all-to-all(f32[8,1,37632]{2,1,0:T(1,128)S(1)} %reshape.1143), channel_id=1, replica_groups=mesh['slab'=8,'pencil'=4] {'slab'}, dimensions={0} | all-to-all | bytes 2408448 | tf_op jit(solution)/shard_map/all_to_all | solution.py:276
  321.6 3.5 reduce.32
  325.2 6.0 reshape.1144
  339.9 3.4 fusion.94
  349.6 5.8 reshape.1145
  355.4 6.8 all-to-all-start.3
  364.3 23.8 %all-to-all-done.3 = f32[4,1,75264]{2,1,0:T(1,128)S(1)} async-done(((f32[4,1,75264]{2,1,0:T(1,128)}), f32[4,1,75264]{2,1,0:T(1,128)S(1)}, u32[]{:S(2)}, u32[]{:S(2)}) %all-to-all-start.3) | async-done | bytes 1204256 | tf_op jit(solution)/shard_map/all_to_all | solution.py:281
  388.1 4.1 reduce.33
  392.2 6.1 reshape.1146
  398.3 6.4 copy.163
  404.8 4.5 all_to_all.54
  409.3 4.0 convolution_bitcast_fusion
  416.1 6.5 collective-permute-done.4
  426.7 44.4 %psum.7 = f32[]{:T(128)} all-reduce(f32[]{:T(128)S(6)} %mul_shard_map.3), channel_id=1, replica_groups=mesh['slab'=8,'pencil'=4] {'slab','pencil'}, use_global_device_ids=true, to_apply=%region_17.18 | all-reduce | flops 1 | bytes 8 | tf_op jit(solution)/shard_map/psum | solution.py:272
  473.4 293.6 %while.40 = (s32[]{:T(128)}, f32[4,3,768]{2,1,0:T(4,128)S(1)}, f32[4,768,12]{1,2,0:T(8,128)}, f32[4,768,56]{1,2,0:T(8,128)}, f32[4,768,384]{2,1,0:T(8,128)}, /*i...) while((s32[]{:T(128)}, f32[4,3,768]{2,1,0:T(4,128)S(1)}, ...), condition=%wide.region_19.20_spmd, body=%wide.region_18.19_spmd.sunk | while | flops 4775567872 | bytes 50012400 | solution.py:301
  478.4 6.7 fusion.381
  489.8 7.0 copy.181
  499.6 12.6 %fusion.384 = f32[768,1,12]{2,1,0:T(1,128)} fusion(f32[768,56,1]{1,2,0:T(1,128)S(1)} %bitcast.336, f32[768,56,12]{1,2,0:T(8,128)} %copy.181), kind=kOutput, calls=%fused_computation.483.clone.1 | convolution fusion | flops 6193152 | bytes 2273280 | tf_op jit(solution)/shard_map/while/body/eval_jaxpr/sz,sy,syz->s/dot_general | solution.py:298
  514.0 7.0 copy.179
  521.2 12.0 %fusion.383 = f32[768,1,12]{2,1,0:T(1,128)S(1)} fusion(f32[768,56,1]{1,2,0:T(1,128)S(1)} %bitcast.339, f32[768,56,12]{1,2,0:T(8,128)} %copy.179), kind=kOutput, calls=%fused_computation.482.clone.1 | convolution fusion | flops 6193152 | bytes 2273280 | tf_op jit(solution)/shard_map/while/body/eval_jaxpr/sz,sy,syz->s/dot_general | solution.py:297
  534.5 12.0 %fusion.385 = f32[768,1,12]{2,1,0:T(1,128)S(1)} fusion(f32[768,56,1]{1,2,0:T(1,128)S(1)} %bitcast.337, f32[768,56,12]{1,2,0:T(8,128)} %copy.179), kind=kOutput, calls=%fused_computation.481.clone.1 | convolution fusion | flops 6193152 | bytes 2273280 | tf_op jit(solution)/shard_map/while/body/eval_jaxpr/sz,sy,syz->s/dot_general | solution.py:296
  551.8 6.7 fusion.381
  563.2 7.0 copy.181
  573.0 12.6 %fusion.384 = f32[768,1,12]{2,1,0:T(1,128)} fusion(f32[768,56,1]{1,2,0:T(1,128)S(1)} %bitcast.336, f32[768,56,12]{1,2,0:T(8,128)} %copy.181), kind=kOutput, calls=%fused_computation.483.clone.1 | convolution fusion | flops 6193152 | bytes 2273280 | tf_op jit(solution)/shard_map/while/body/eval_jaxpr/sz,sy,syz->s/dot_general | solution.py:298
  587.4 7.0 copy.179
  594.6 12.0 %fusion.383 = f32[768,1,12]{2,1,0:T(1,128)S(1)} fusion(f32[768,56,1]{1,2,0:T(1,128)S(1)} %bitcast.339, f32[768,56,12]{1,2,0:T(8,128)} %copy.179), kind=kOutput, calls=%fused_computation.482.clone.1 | convolution fusion | flops 6193152 | bytes 2273280 | tf_op jit(solution)/shard_map/while/body/eval_jaxpr/sz,sy,syz->s/dot_general | solution.py:297
  608.0 12.0 %fusion.385 = f32[768,1,12]{2,1,0:T(1,128)S(1)} fusion(f32[768,56,1]{1,2,0:T(1,128)S(1)} %bitcast.337, f32[768,56,12]{1,2,0:T(8,128)} %copy.179), kind=kOutput, calls=%fused_computation.481.clone.1 | convolution fusion | flops 6193152 | bytes 2273280 | tf_op jit(solution)/shard_map/while/body/eval_jaxpr/sz,sy,syz->s/dot_general | solution.py:296
  625.0 6.7 fusion.381
  636.4 7.0 copy.181
  646.2 12.6 %fusion.384 = f32[768,1,12]{2,1,0:T(1,128)} fusion(f32[768,56,1]{1,2,0:T(1,128)S(1)} %bitcast.336, f32[768,56,12]{1,2,0:T(8,128)} %copy.181), kind=kOutput, calls=%fused_computation.483.clone.1 | convolution fusion | flops 6193152 | bytes 2273280 | tf_op jit(solution)/shard_map/while/body/eval_jaxpr/sz,sy,syz->s/dot_general | solution.py:298
  660.6 7.0 copy.179
  667.8 12.0 %fusion.383 = f32[768,1,12]{2,1,0:T(1,128)S(1)} fusion(f32[768,56,1]{1,2,0:T(1,128)S(1)} %bitcast.339, f32[768,56,12]{1,2,0:T(8,128)} %copy.179), kind=kOutput, calls=%fused_computation.482.clone.1 | convolution fusion | flops 6193152 | bytes 2273280 | tf_op jit(solution)/shard_map/while/body/eval_jaxpr/sz,sy,syz->s/dot_general | solution.py:297
  681.2 12.0 %fusion.385 = f32[768,1,12]{2,1,0:T(1,128)S(1)} fusion(f32[768,56,1]{1,2,0:T(1,128)S(1)} %bitcast.337, f32[768,56,12]{1,2,0:T(8,128)} %copy.179), kind=kOutput, calls=%fused_computation.481.clone.1 | convolution fusion | flops 6193152 | bytes 2273280 | tf_op jit(solution)/shard_map/while/body/eval_jaxpr/sz,sy,syz->s/dot_general | solution.py:296
  698.2 6.7 fusion.381
  709.6 7.0 copy.181
  719.4 12.6 %fusion.384 = f32[768,1,12]{2,1,0:T(1,128)} fusion(f32[768,56,1]{1,2,0:T(1,128)S(1)} %bitcast.336, f32[768,56,12]{1,2,0:T(8,128)} %copy.181), kind=kOutput, calls=%fused_computation.483.clone.1 | convolution fusion | flops 6193152 | bytes 2273280 | tf_op jit(solution)/shard_map/while/body/eval_jaxpr/sz,sy,syz->s/dot_general | solution.py:298
  733.8 7.0 copy.179
  741.0 12.0 %fusion.383 = f32[768,1,12]{2,1,0:T(1,128)S(1)} fusion(f32[768,56,1]{1,2,0:T(1,128)S(1)} %bitcast.339, f32[768,56,12]{1,2,0:T(8,128)} %copy.179), kind=kOutput, calls=%fused_computation.482.clone.1 | convolution fusion | flops 6193152 | bytes 2273280 | tf_op jit(solution)/shard_map/while/body/eval_jaxpr/sz,sy,syz->s/dot_general | solution.py:297
  754.4 12.0 %fusion.385 = f32[768,1,12]{2,1,0:T(1,128)S(1)} fusion(f32[768,56,1]{1,2,0:T(1,128)S(1)} %bitcast.337, f32[768,56,12]{1,2,0:T(8,128)} %copy.179), kind=kOutput, calls=%fused_computation.481.clone.1 | convolution fusion | flops 6193152 | bytes 2273280 | tf_op jit(solution)/shard_map/while/body/eval_jaxpr/sz,sy,syz->s/dot_general | solution.py:296
  769.7 5.5 convolution_convert_fusion
  (339 shorter events, 197.1 us)
Async XLA Ops:
  0.6 1.6 copy-start
  2.3 4.2 copy-start.8
  6.4 1.6 copy-start.3
  8.1 1.6 copy-start.13
  8.1 1.6 copy-start.16
  8.1 1.6 copy-start.20
  8.4 1.2 copy-start.2
  9.6 1.2 copy-start.15
  9.6 1.4 copy-start.18
  9.6 1.4 copy-start.21
  9.6 1.4 copy-start.22
  9.7 1.5 copy-start.23
  13.4 1.9 copy-start.24
  31.3 7.0 copy-start.25
  38.4 1.9 copy-start.24
  56.4 7.0 copy-start.25
  63.4 1.9 copy-start.24
  81.4 7.0 copy-start.25
  88.4 1.9 copy-start.24
  106.3 7.1 copy-start.25
  113.4 5.3 copy-start.10
  114.6 10.5 %collective-permute-start = (f32[4,56,384]{2,1,0:T(8,128)S(1)}, f32[4,56,384]{2,1,0:T(8,128)S(1)}, u32[]{:S(2)}, u32[]{:S(2)}) collective-permute-start(f32[4,56,384]{2,1,0:T(8,128)S(1)} %get-tuple-element.502), channel_id=1, source_target_pairs={{0,4},{4,8},{8,12},{12,16},{16,20},{20,24},{24,28},{28,0},{1,5},{5... | collective-permute-start | bytes 1032200 | tf_op jit(solution)/shard_map/ppermute | solution.py:26
  114.7 11.5 %collective-permute-start.1 = (f32[4,56,384]{2,1,0:T(8,128)S(1)}, f32[4,56,384]{2,1,0:T(8,128)S(1)}, u32[]{:S(2)}, u32[]{:S(2)}) collective-permute-start(f32[4,56,384]{2,1,0:T(8,128)S(1)} %get-tuple-element.501), channel_id=1, source_target_pairs={{4,0},{8,4},{12,8},{16,12},{20,16},{24,20},{28,24},{0,28},{5,1},{9... | collective-permute-start | bytes 1032200 | tf_op jit(solution)/shard_map/ppermute | solution.py:28
  126.3 4.7 collective-permute-start.2
  129.3 4.9 collective-permute-start.3
  145.6 5.9 copy-start.19
  145.6 29.4 %all-to-all-start = ((f32[4,1,75264]{2,1,0:T(1,128)}), f32[4,1,75264]{2,1,0:T(1,128)S(1)}, u32[]{:S(2)}, u32[]{:S(2)}) async-start(f32[4,1,75264]{2,1,0:T(1,128)} %reshape.1139), calls=%async_computation | async-start | bytes 2408448 | tf_op jit(solution)/shard_map/all_to_all | solution.py:252
  218.0 21.5 %all-to-all-start.1 = ((f32[8,1,37632]{2,1,0:T(1,128)}), f32[8,1,37632]{2,1,0:T(1,128)S(1)}, u32[]{:S(2)}, u32[]{:S(2)}) async-start(f32[8,1,37632]{2,1,0:T(1,128)} %reshape.1141), calls=%async_computation.1 | async-start | bytes 2408448 | tf_op jit(solution)/shard_map/all_to_all | solution.py:255
  289.7 3.6 copy-start.6
  289.7 4.4 copy-start.5
  355.4 32.6 %all-to-all-start.3 = ((f32[4,1,75264]{2,1,0:T(1,128)}), f32[4,1,75264]{2,1,0:T(1,128)S(1)}, u32[]{:S(2)}, u32[]{:S(2)}) async-start(f32[4,1,75264]{2,1,0:T(1,128)} %reshape.1145), calls=%async_computation.3 | async-start | bytes 2408448 | tf_op jit(solution)/shard_map/all_to_all | solution.py:281
  404.8 4.5 copy-start.7
  413.3 13.4 %copy-start.11 = (f32[4,768]{1,0:T(4,128)S(1)}, f32[4,768]{1,0:T(4,128)}, u32[]{:S(2)}) copy-start(f32[4,768]{1,0:T(4,128)} %get-tuple-element.850) | copy-start | bytes 36868
  413.4 9.2 %collective-permute-start.4 = (f32[48,4,384]{2,1,0:T(4,128)S(1)}, f32[48,4,384]{2,1,0:T(4,128)S(1)}, u32[]{:S(2)}, u32[]{:S(2)}) collective-permute-start(f32[48,4,384]{2,1,0:T(4,128)S(1)} %get-tuple-element.517), channel_id=1, source_target_pairs={{0,4},{4,8},{8,12},{12,16},{16,20},{20,24},{24,28},{28,0},{1,5},{5... | collective-permute-start | bytes 884744 | tf_op jit(solution)/shard_map/ppermute | solution.py:26
  413.5 9.1 %collective-permute-start.5 = (f32[48,4,384]{2,1,0:T(4,128)S(1)}, f32[48,4,384]{2,1,0:T(4,128)S(1)}, u32[]{:S(2)}, u32[]{:S(2)}) collective-permute-start(f32[48,4,384]{2,1,0:T(4,128)S(1)} %get-tuple-element.518), channel_id=1, source_target_pairs={{4,0},{8,4},{12,8},{16,12},{20,16},{24,20},{28,24},{0,28},{5,1},{9... | collective-permute-start | bytes 884744 | tf_op jit(solution)/shard_map/ppermute | solution.py:28
  422.6 49.1 %collective-permute-start.6 = (f32[4,24,384]{2,1,0:T(8,128)S(1)}, f32[4,24,384]{2,1,0:T(8,128)S(1)}, u32[]{:S(2)}, u32[]{:S(2)}) collective-permute-start(f32[4,24,384]{2,1,0:T(8,128)S(1)} %get-tuple-element.503), channel_id=1, source_target_pairs={{0,1},{1,2},{2,3},{3,0},{4,5},{5,6},{6,7},{7,4},{8,9},{9,10},{10,1... | collective-permute-start | bytes 442376 | tf_op jit(solution)/shard_map/ppermute | solution.py:26
  424.2 47.6 %collective-permute-start.7 = (f32[4,24,384]{2,1,0:T(8,128)S(1)}, f32[4,24,384]{2,1,0:T(8,128)S(1)}, u32[]{:S(2)}, u32[]{:S(2)}) collective-permute-start(f32[4,24,384]{2,1,0:T(8,128)S(1)} %get-tuple-element.504), channel_id=1, source_target_pairs={{1,0},{2,1},{3,2},{0,3},{5,4},{6,5},{7,6},{4,7},{9,8},{10,9},{11,1... | collective-permute-start | bytes 442376 | tf_op jit(solution)/shard_map/ppermute | solution.py:28
  473.3 293.8 %copy-start.12 = (f32[1536,3]{0,1:T(4,128)S(1)}, f32[1536,3]{0,1:T(4,128)}, u32[]{:S(2)}) copy-start(f32[1536,3]{0,1:T(4,128)} %get-tuple-element.530) | copy-start | bytes 55300
  473.4 293.8 %copy-start.17 = (bf16[3,256]{1,0:T(4,128)(2,1)S(1)}, bf16[3,256]{1,0:T(4,128)(2,1)}, u32[]{:S(2)}) copy-start(bf16[3,256]{1,0:T(4,128)(2,1)} %param.37) | copy-start | bytes 4612
  521.2 13.1 %copy-start.1 = (f32[768,1,12]{2,1,0:T(1,128)S(1)}, f32[768,1,12]{2,1,0:T(1,128)}, u32[]{:S(2)}) copy-start(f32[768,1,12]{2,1,0:T(1,128)} %fusion.384) | copy-start | bytes 110596 | tf_op jit(solution)/shard_map/while
  594.6 13.1 %copy-start.1 = (f32[768,1,12]{2,1,0:T(1,128)S(1)}, f32[768,1,12]{2,1,0:T(1,128)}, u32[]{:S(2)}) copy-start(f32[768,1,12]{2,1,0:T(1,128)} %fusion.384) | copy-start | bytes 110596 | tf_op jit(solution)/shard_map/while
  667.8 13.1 %copy-start.1 = (f32[768,1,12]{2,1,0:T(1,128)S(1)}, f32[768,1,12]{2,1,0:T(1,128)}, u32[]{:S(2)}) copy-start(f32[768,1,12]{2,1,0:T(1,128)} %fusion.384) | copy-start | bytes 110596 | tf_op jit(solution)/shard_map/while
  741.0 13.1 %copy-start.1 = (f32[768,1,12]{2,1,0:T(1,128)S(1)}, f32[768,1,12]{2,1,0:T(1,128)}, u32[]{:S(2)}) copy-start(f32[768,1,12]{2,1,0:T(1,128)} %fusion.384) | copy-start | bytes 110596 | tf_op jit(solution)/shard_map/while
  767.1 2.6 copy-start.14
  767.6 2.1 copy-start.4
  767.6 2.1 copy-start.9
